TPU v7x, 256 devices: a whole 4x4x8 slice. The times are simulated.
256 devices in a mesh: hyp: 32 (over y, x, core), head: 8 (over z).
Axes of the slice: x: 4, y: 4, z: 8, core: 2. Of those that a mesh axis runs over, the one named last changes fastest.
Arguments:
- step_embeds: bfloat16 [3, 512, 4096], P(None, 'hyp'), may hold values from -6 to 6
- lang_table: bfloat16 [8, 4096], replicated, may hold values from -3 to 3
- lang_ids: int32 [32, 4], replicated, may hold values from 0 to 7
- self_gain: float32 [4096], replicated, may hold values from 0.1 to 1.9
- self_wq: bfloat16 [4096, 2048], P(None, 'head'), may hold values from -0.09375 to 0.09375
- self_wk: bfloat16 [4096, 2048], P(None, 'head'), may hold values from -0.09375 to 0.09375
- self_wv: bfloat16 [4096, 2048], P(None, 'head'), may hold values from -0.09375 to 0.09375
- self_wo: bfloat16 [2048, 4096], P('head'), may hold values from -0.125 to 0.125
- cross_gain: float32 [4096], replicated, may hold values from 0.1 to 1.9
- cross_wq: bfloat16 [4096, 2048], P(None, 'head'), may hold values from -0.09375 to 0.09375
- cross_wkv: bfloat16 [4096, 4096], P('hyp', 'head'), may hold values from -0.09375 to 0.09375
- encoder_rows: bfloat16 [24576, 4096], P('hyp', 'head'), may hold values from -200 to 200
- doc_lengths: int32 [32], P('hyp'), may hold values from 192 to 768, as said below
- past_keys: bfloat16 [512, 32, 2048], P('hyp', None, 'head'), may hold values from -200 to 200
- past_values: bfloat16 [512, 32, 2048], P('hyp', None, 'head'), may hold values from -6 to 6
- parents: int32 [3, 512], replicated, may hold values from 0 to 3
Outputs:
- cross_context: bfloat16 [3, 512, 2048], P(None, 'hyp', 'head')
- final_keys: bfloat16 [512, 35, 2048], P('hyp', None, 'head')
- final_values: bfloat16 [512, 35, 2048], P('hyp', None, 'head')
Inputs may be any that keep to these rules, and one draw needn't show every extreme that they name: `doc_lengths`: some document has exactly 768 live rows. `parents`: A parent is a beam of the same document and target.
All inputs are finite; a program needn't handle non-finite values.
Results may differ from a plain program's by a relative error of at most 0.03.
Values may be sent and summed in bfloat16 or wider, within the bound.
No kernel may reach another device: no remote copies, remote signals or barrier semaphores. Data moves between devices by JAX's collectives and lax.ppermute only.
A program may use at most 128 MiB of HBM per device.

v0:
```python
import jax
import jax.numpy as jnp
from jax import lax
from jax.sharding import PartitionSpec as P

HEAD = 256
BEAMS = 4
TARGETS = 4
STEPS = 3
EPSILON = 1e-06


def shifted(block, axis, distance):
    devices = range(lax.axis_size(axis))
    route = [((i - distance) % len(devices), i) for i in devices]
    return lax.ppermute(block, axis, route)


def rms_scaled(values_in, gain):
    mean_square = jnp.mean(values_in * values_in, axis=-1, keepdims=True)
    return values_in * lax.rsqrt(mean_square + EPSILON) * gain


def pick_rows(candidates, selector, row_axis):
    shape_list = [1] * candidates[0].ndim
    shape_list[row_axis] = selector.shape[0]
    chosen = candidates[0]
    for position in range(1, len(candidates)):
        chosen = jnp.where((selector == position).reshape(shape_list), candidates[position], chosen)
    return chosen


def partial_attend(queries, cache_stack, scaling):
    row_count = cache_stack.shape[1]
    cached = cache_stack.shape[2]
    heads_here = cache_stack.shape[3] // HEAD
    key_part = cache_stack[0].reshape(row_count, cached, heads_here, HEAD)
    value_part = cache_stack[1].reshape(row_count, cached, heads_here, HEAD).astype(jnp.float32)
    scores = (
        jnp.einsum(
            "rhd,rphd->rhp",
            queries.reshape(row_count, heads_here, HEAD),
            key_part,
            preferred_element_type=jnp.float32,
        )
        * scaling
    )
    highest = jnp.max(scores, axis=2)
    raw_weights = jnp.exp(scores - highest[:, :, None])
    totals = jnp.sum(raw_weights, axis=2)
    summed = jnp.einsum("rhp,rphd->rhd", raw_weights, value_part)
    return (highest, totals, summed)


def cross_attend(queries, cross_keys, cross_values, doc_length, scaling):
    query_rows = queries.shape[0]
    heads_here = cross_keys.shape[1]
    scores = (
        jnp.einsum(
            "qhd,jhd->hqj",
            queries.reshape(query_rows, heads_here, HEAD),
            cross_keys,
            preferred_element_type=jnp.float32,
        )
        * scaling
    )
    live_mask = lax.broadcasted_iota(jnp.int32, (1, 1, cross_keys.shape[0]), 2) < doc_length
    scores = jnp.where(live_mask, scores, -jnp.inf)
    highest = jnp.max(scores, axis=2, keepdims=True)
    raw_weights = jnp.exp(scores - highest)
    totals = jnp.sum(raw_weights, axis=2, keepdims=True)
    weights = (raw_weights / totals).astype(jnp.bfloat16)
    output = jnp.einsum("hqj,jhd->qhd", weights, cross_values, preferred_element_type=jnp.float32)
    return output.reshape(query_rows, heads_here * HEAD).astype(jnp.bfloat16)


def shards(
    step_embeds,
    lang_table,
    lang_ids,
    self_gain,
    self_wq,
    self_wk,
    self_wv,
    self_wo,
    cross_gain,
    cross_wq,
    cross_wkv,
    encoder_rows,
    doc_lengths,
    past_keys,
    past_values,
    parents,
):
    hyp_count = lax.axis_size("hyp")
    group_size = hyp_count // BEAMS
    my_index = lax.axis_index("hyp")
    my_beam = my_index // group_size
    my_slot = my_index % group_size
    row_count = step_embeds.shape[1]
    head_width = self_wq.shape[1]
    heads_here = head_width // HEAD
    doc_count = lang_ids.shape[0]
    scaling = HEAD ** (-0.5)
    my_langs = lax.dynamic_slice_in_dim(lang_ids, my_slot * BEAMS, BEAMS, 0).reshape(row_count)
    one_hot = (
        my_langs[:, None] == lax.broadcasted_iota(jnp.int32, (1, lang_table.shape[0]), 1)
    ).astype(jnp.bfloat16)
    lang_rows = jnp.dot(one_hot, lang_table, preferred_element_type=jnp.float32)
    full_weights = lax.all_gather(cross_wkv, "hyp", axis=0, tiled=True)
    cross_kv = jnp.dot(
        lax.all_gather(encoder_rows, "head", axis=1, tiled=True),
        full_weights,
        preferred_element_type=jnp.float32,
    ).astype(jnp.bfloat16)
    cross_kv = cross_kv.reshape(encoder_rows.shape[0], heads_here, 2, HEAD)
    cross_keys = cross_kv[:, :, 0, :]
    cross_values = cross_kv[:, :, 1, :]
    doc_length = doc_lengths[0]
    parent_view = parents.reshape(parents.shape[0], BEAMS, -1)
    my_parents = lax.dynamic_slice_in_dim(parent_view, my_slot * row_count, row_count, 2)
    own_parents = lax.dynamic_index_in_dim(my_parents, my_beam, 1, keepdims=False)
    contexts = []
    cache_stack = jnp.stack([past_keys, past_values])
    for step_idx in range(STEPS):
        offsets = (my_beam - own_parents[step_idx]) % BEAMS
        moved_list = [cache_stack]
        for peer_hop in range(1, BEAMS):
            moved_list.append(shifted(cache_stack, "hyp", peer_hop * group_size))
        cache_stack = pick_rows(moved_list, offsets, 1)
        start_hidden_in = step_embeds[step_idx].astype(jnp.float32) + lang_rows
        normed = rms_scaled(start_hidden_in, self_gain).astype(jnp.bfloat16)
        new_query = jnp.dot(normed, self_wq, preferred_element_type=jnp.float32).astype(
            jnp.bfloat16
        )
        new_key = jnp.dot(normed, self_wk, preferred_element_type=jnp.float32).astype(jnp.bfloat16)
        new_value = jnp.dot(normed, self_wv, preferred_element_type=jnp.float32).astype(
            jnp.bfloat16
        )
        fresh_rows = jnp.stack([new_key, new_value])[:, :, None, :]
        hidden_in, new_query, fresh_rows = (start_hidden_in, new_query, fresh_rows)
        cache_stack = jnp.concatenate([cache_stack, fresh_rows], axis=2)
        attn_parts = partial_attend(new_query, cache_stack, scaling)
        rows_here = hidden_in.shape[0]
        self_context = (
            (attn_parts[2] / attn_parts[1][:, :, None])
            .reshape(rows_here, head_width)
            .astype(jnp.bfloat16)
        )
        partial_out = jnp.dot(self_context, self_wo, preferred_element_type=jnp.float32)
        residual = hidden_in + lax.psum(partial_out.astype(jnp.bfloat16), "head").astype(
            jnp.float32
        )
        normed_cross = rms_scaled(residual, cross_gain).astype(jnp.bfloat16)
        cross_query = jnp.dot(normed_cross, cross_wq, preferred_element_type=jnp.float32).astype(
            jnp.bfloat16
        )
        every_query = lax.all_gather(cross_query, "hyp", axis=0, tiled=True)
        arranged = every_query.reshape(BEAMS, doc_count, TARGETS, head_width)
        doc_queries = lax.dynamic_index_in_dim(arranged, my_index, 1, keepdims=False)
        answer = cross_attend(
            doc_queries.reshape(BEAMS * TARGETS, head_width),
            cross_keys,
            cross_values,
            doc_length,
            scaling,
        )
        every_answer = lax.all_gather(answer, "hyp", axis=0, tiled=True)
        by_owner = every_answer.reshape(doc_count, BEAMS, TARGETS, head_width)
        my_block = lax.dynamic_slice_in_dim(by_owner, my_slot * BEAMS, BEAMS, 0)
        contexts.append(
            lax.dynamic_index_in_dim(my_block, my_beam, 1, keepdims=False).reshape(
                row_count, head_width
            )
        )
    return (jnp.stack(contexts), cache_stack[0], cache_stack[1])


def solution(mesh):
    return jax.shard_map(
        shards,
        mesh=mesh,
        in_specs=(
            P(None, "hyp", None),
            P(),
            P(),
            P(),
            P(None, "head"),
            P(None, "head"),
            P(None, "head"),
            P("head", None),
            P(),
            P(None, "head"),
            P("hyp", "head"),
            P("hyp", "head"),
            P("hyp"),
            P("hyp", None, "head"),
            P("hyp", None, "head"),
            P(),
        ),
        out_specs=(P(None, "hyp", "head"), P("hyp", None, "head"), P("hyp", None, "head")),
        check_vma=False,
    )
```

profile of v0, /device:TPU:1, one launch (start us, length us, event | category | flops | bytes accessed | tf_op | source)
XLA Modules:
  0.0 360.1 jit_solution(13073119696567710992)
XLA Ops:
  8.1 1.5 copy_bitcast_fusion
  9.6 0.8 pad_maximum_fusion.2
  10.4 3.6 collective-permute-start
  14.0 0.3 collective-permute-start.1
  14.3 0.7 collective-permute-start.2
  15.3 0.4 multiply_reduce_fusion.1
  15.9 2.7 fusion.11
  18.6 1.0 fusion.10
  19.6 0.4 fusion.8
  20.0 0.4 fusion.7
  20.4 1.0 fusion.5
  21.4 1.0 fusion.4
  22.4 2.8 fusion.9
  25.2 1.0 fusion.3
  26.2 0.4 fusion.6
  26.6 0.3 copy-done.21
  27.1 8.9 %collective-permute-done = bf16[2,16,32,256]{3,1,2,0:T(8,128)(2,1)} collective-permute-done((bf16[2,16,32,256]{3,1,2,0:T(8,128)(2,1)}, bf16[2,16,32,256]{3,1,2,0:T(8,128)(2,1)}, u32[]{:S(2)}, u32[]{:S(2)}) %collective-permute-start) | collective-permute-done | bytes 524320 | tf_op jit(solution)/shard_map/ppermute | solution.py:16
  36.0 4.9 %collective-permute-done.2 = bf16[2,16,32,256]{3,1,2,0:T(8,128)(2,1)} collective-permute-done((bf16[2,16,32,256]{3,1,2,0:T(8,128)(2,1)}, bf16[2,16,32,256]{3,1,2,0:T(8,128)(2,1)}, u32[]{:S(2)}, u32[]{:S(2)}) %collective-permute-start.2) | collective-permute-done | bytes 524320 | tf_op jit(solution)/shard_map/ppermute | solution.py:16
  40.9 1.5 select_select_fusion.2
  42.6 0.4 collective-permute-start.4
  43.0 1.0 collective-permute-start.5
  44.6 0.2 fusion.23
  44.8 1.1 convolution_convert_fusion.2
  45.9 10.0 %collective-permute-done.3 = bf16[2,16,33,256]{3,1,2,0:T(8,128)(2,1)S(1)} collective-permute-done((bf16[2,16,33,256]{3,1,2,0:T(8,128)(2,1)S(1)}, bf16[2,16,33,256]{3,1,2,0:T(8,128)(2,1)S(1)}, u32[]{:S(2)}, u32[]{:S(2)}) %collective-permute-start.3) | collective-permute-done | bytes 540704 | tf_op jit(solution)/shard_map/ppermute | solution.py:16
  55.9 1.1 collective-permute-done.4
  57.0 12.9 %collective-permute-done.5 = bf16[2,16,33,256]{3,1,2,0:T(8,128)(2,1)S(1)} collective-permute-done((bf16[2,16,33,256]{3,1,2,0:T(8,128)(2,1)S(1)}, bf16[2,16,33,256]{3,1,2,0:T(8,128)(2,1)S(1)}, u32[]{:S(2)}, u32[]{:S(2)}) %collective-permute-start.5) | collective-permute-done | bytes 540704 | tf_op jit(solution)/shard_map/ppermute | solution.py:16
  70.2 0.4 collective-permute-start.7
  70.7 1.0 collective-permute-start.8
  72.3 0.2 fusion.19
  72.5 1.1 convolution_convert_fusion.1
  73.6 10.3 %collective-permute-done.6 = bf16[2,16,34,256]{3,1,2,0:T(8,128)(2,1)S(1)} collective-permute-done((bf16[2,16,34,256]{3,1,2,0:T(8,128)(2,1)S(1)}, bf16[2,16,34,256]{3,1,2,0:T(8,128)(2,1)S(1)}, u32[]{:S(2)}, u32[]{:S(2)}) %collective-permute-start.6) | collective-permute-done | bytes 557088 | tf_op jit(solution)/shard_map/ppermute | solution.py:16
  83.9 0.7 collective-permute-done.7
  84.6 13.7 %collective-permute-done.8 = bf16[2,16,34,256]{3,1,2,0:T(8,128)(2,1)S(1)} collective-permute-done((bf16[2,16,34,256]{3,1,2,0:T(8,128)(2,1)S(1)}, bf16[2,16,34,256]{3,1,2,0:T(8,128)(2,1)S(1)}, u32[]{:S(2)}, u32[]{:S(2)}) %collective-permute-start.8) | collective-permute-done | bytes 557088 | tf_op jit(solution)/shard_map/ppermute | solution.py:16
  98.6 0.2 fusion.17
  99.3 0.2 fusion.15
  99.5 1.1 convolution_convert_fusion
  100.7 0.5 all-gather.8.cloned.1.call-update
  101.2 0.5 all-gather.6.cloned.1.call-update
  102.4 0.6 iota_compare_fusion.2
  103.0 72.8 %all-reduce.3.cloned.1.call-done = (bf16[16,4096]{1,0:T(8,128)(2,1)}, bf16[16,4096]{1,0:T(8,128)(2,1)}, bf16[16,4096]{1,0:T(8,128)(2,1)}) async-done(((bf16[16,4096]{1,0:T(8,128)(2,1)}, bf16[16,4096]{1,0:T(8,128)(2,1)}, bf16[16,4096]{1,0:T(8,128)(2,1)}), (bf16[16,4096]{1,0:T(8,128)(2,1)}, bf16[16,4096]{1,0:T(8,128)(2,1)}, bf16[16,4096]{1,0:T(8,128)(2,1)})) %all-reduce.3.cloned.1.call-update) | async-done | bytes 393232 | tf_op jit(solution)/shard_map/psum | solution.py:151
  175.8 1.8 multiply_reduce_fusion.4
  177.6 2.1 convolution_convert_fusion.4
  179.7 37.9 %all_gather.30 = bf16[512,256]{1,0:T(8,128)(2,1)S(1)} all-gather(bf16[16,256]{1,0:T(8,128)(2,1)S(1)} %convolution_convert_fusion.4), channel_id=1, replica_groups=mesh['hyp'=32,'head'=8] {'hyp'}, dimensions={0}, use_global_device_ids=true | all-gather | bytes 270336 | tf_op jit(solution)/shard_map/all_gather | solution.py:158
  217.7 0.6 reshape.403
  218.3 0.6 add_rsqrt_fusion.2
  218.9 2.0 convolution_convert_fusion.8
  220.9 24.2 %all_gather.28 = bf16[512,256]{1,0:T(8,128)(2,1)S(1)} all-gather(bf16[16,256]{1,0:T(8,128)(2,1)S(1)} %convolution_convert_fusion.8), channel_id=1, replica_groups=mesh['hyp'=32,'head'=8] {'hyp'}, dimensions={0}, use_global_device_ids=true | all-gather | bytes 270336 | tf_op jit(solution)/shard_map/all_gather | solution.py:158
  245.2 0.6 reshape.398
  245.8 2.0 convolution_convert_fusion.12
  247.8 22.6 %all_gather.26 = bf16[512,256]{1,0:T(8,128)(2,1)S(1)} all-gather(bf16[16,256]{1,0:T(8,128)(2,1)S(1)} %convolution_convert_fusion.12), channel_id=1, replica_groups=mesh['hyp'=32,'head'=8] {'hyp'}, dimensions={0}, use_global_device_ids=true | all-gather | bytes 270336 | tf_op jit(solution)/shard_map/all_gather | solution.py:158
  270.7 7.5 %convolution_convert_fusion.3 = bf16[768,512]{0,1:T(8,128)(2,1)S(1)} fusion(bf16[768,4096]{1,0:T(8,128)(2,1)} %all-gather.6.cloned.1.call-done, bf16[4096,512]{1,0:T(8,128)(2,1)} %all-gather.8.cloned.1.call-done), kind=kOutput, calls=%fused_computation.3 | convolution fusion | flops 3221618688 | bytes 11272192 | tf_op jit(solution)/shard_map/dot_general | solution.py:111
  278.2 0.3 fusion.77
  278.5 0.2 fusion.46
  278.7 0.2 fusion.14
  278.9 24.5 %all-gather.2 = bf16[512,1,256]{2,0,1:T(8,128)(2,1)S(1)} all-gather(bf16[16,1,256]{2,0,1:T(8,128)(2,1)S(1)} %fusion.14), channel_id=4, replica_groups=mesh['hyp'=32,'head'=8] {'hyp'}, dimensions={0}, use_global_device_ids=true | all-gather | bytes 270336 | tf_op jit(solution)/shard_map/all_gather | solution.py:168
  303.5 0.3 fusion.78
  303.8 0.2 fusion.45
  304.0 0.2 fusion.13
  304.2 22.7 %all-gather.1 = bf16[512,1,256]{2,0,1:T(8,128)(2,1)S(1)} all-gather(bf16[16,1,256]{2,0,1:T(8,128)(2,1)S(1)} %fusion.13), channel_id=3, replica_groups=mesh['hyp'=32,'head'=8] {'hyp'}, dimensions={0}, use_global_device_ids=true | all-gather | bytes 270336 | tf_op jit(solution)/shard_map/all_gather | solution.py:168
  327.0 0.3 fusion.79
  327.3 0.2 fusion.44
  327.5 0.2 fusion.12
  327.7 24.3 %all-gather = bf16[512,1,256]{2,0,1:T(8,128)(2,1)S(1)} all-gather(bf16[16,1,256]{2,0,1:T(8,128)(2,1)S(1)} %fusion.12), channel_id=2, replica_groups=mesh['hyp'=32,'head'=8] {'hyp'}, dimensions={0}, use_global_device_ids=true | all-gather | bytes 270336 | tf_op jit(solution)/shard_map/all_gather | solution.py:168
  352.0 0.6 pad_maximum_fusion.4
  (105 shorter events, 3.6 us)
Async XLA Ops:
  8.0 36.8 %copy-start = (bf16[256,4096]{1,0:T(8,128)(2,1)S(1)}, bf16[256,4096]{1,0:T(8,128)(2,1)}, u32[]{:S(2)}) copy-start(bf16[256,4096]{1,0:T(8,128)(2,1)} %param.23) | copy-start | bytes 6291460
  8.0 7.0 %copy-start.22 = (s32[32,4]{0,1:T(4,128)S(1)}, s32[32,4]{0,1:T(4,128)}, u32[]{:S(2)}) copy-start(s32[32,4]{0,1:T(4,128)} %param.18) | copy-start | bytes 1540
  8.0 7.2 %copy-start.4 = (bf16[3,16,4096]{2,1,0:T(8,128)(2,1)S(1)}, bf16[3,16,4096]{2,1,0:T(8,128)(2,1)}, u32[]{:S(2)}) copy-start(bf16[3,16,4096]{2,1,0:T(8,128)(2,1)} %param.16) | copy-start | bytes 1179652
  8.0 7.2 %copy-start.24 = (bf16[8,4096]{1,0:T(8,128)(2,1)S(1)}, bf16[8,4096]{1,0:T(8,128)(2,1)}, u32[]{:S(2)}) copy-start(bf16[8,4096]{1,0:T(8,128)(2,1)} %param.17) | copy-start | bytes 196612
  8.0 7.7 %copy-start.17 = (f32[4096]{0:T(1024)S(1)}, f32[4096]{0:T(1024)}, u32[]{:S(2)}) copy-start(f32[4096]{0:T(1024)} %param.19) | copy-start | bytes 49156
  8.1 167.7 %all-reduce.3.cloned.1.call-start = ((), (), s32[]{:S(2)}) async-start(), calls=%async_computation.2 | async-start | bytes 786432 | tf_op jit(solution)/shard_map/psum | solution.py:151
  10.4 25.6 %collective-permute-start = (bf16[2,16,32,256]{3,1,2,0:T(8,128)(2,1)}, bf16[2,16,32,256]{3,1,2,0:T(8,128)(2,1)}, u32[]{:S(2)}, u32[]{:S(2)}) collective-permute-start(bf16[2,16,32,256]{3,1,2,0:T(8,128)(2,1)} %pad_maximum_fusion.2), channel_id=1, source_target_pairs={{64,0},{72,8},{80,16},{88,24},{96,32},{104,40},{112,48},{120,56},{... | collective-permute-start | bytes 1572872 | tf_op jit(solution)/shard_map/ppermute | solution.py:16
  14.0 22.0 %collective-permute-start.1 = (bf16[2,16,32,256]{3,1,2,0:T(8,128)(2,1)}, bf16[2,16,32,256]{3,1,2,0:T(8,128)(2,1)}, u32[]{:S(2)}, u32[]{:S(2)}) collective-permute-start(bf16[2,16,32,256]{3,1,2,0:T(8,128)(2,1)} %pad_maximum_fusion.2), channel_id=1, source_target_pairs={{128,0},{136,8},{144,16},{152,24},{160,32},{168,40},{176,48},{184,... | collective-permute-start | bytes 1572872 | tf_op jit(solution)/shard_map/ppermute | solution.py:16
  14.3 26.6 %collective-permute-start.2 = (bf16[2,16,32,256]{3,1,2,0:T(8,128)(2,1)}, bf16[2,16,32,256]{3,1,2,0:T(8,128)(2,1)}, u32[]{:S(2)}, u32[]{:S(2)}) collective-permute-start(bf16[2,16,32,256]{3,1,2,0:T(8,128)(2,1)} %pad_maximum_fusion.2), channel_id=1, source_target_pairs={{192,0},{200,8},{208,16},{216,24},{224,32},{232,40},{240,48},{248,... | collective-permute-start | bytes 1572872 | tf_op jit(solution)/shard_map/ppermute | solution.py:16
  15.3 3.4 copy-start.2
  15.9 3.7 %copy-start.5 = (bf16[16,4096]{1,0:T(8,128)(2,1)}, bf16[16,4096]{1,0:T(8,128)(2,1)S(1)}, u32[]{:S(2)}) copy-start(bf16[16,4096]{1,0:T(8,128)(2,1)S(1)} %get-tuple-element.24) | copy-start | bytes 393220
  15.9 3.7 %copy-start.1 = (bf16[4096,256]{1,0:T(8,128)(2,1)S(1)}, bf16[4096,256]{1,0:T(8,128)(2,1)}, u32[]{:S(2)}) copy-start(bf16[4096,256]{1,0:T(8,128)(2,1)} %param.22) | copy-start | bytes 6291460
  22.4 2.8 copy-start.3
  26.2 0.7 copy-start.21
  26.2 0.8 copy-start.15
  26.2 0.8 copy-start.16
  26.2 0.9 copy-start.13
  26.2 0.9 copy-start.14
  40.9 3.2 copy-start.20
  42.5 13.4 %collective-permute-start.3 = (bf16[2,16,33,256]{3,1,2,0:T(8,128)(2,1)S(1)}, bf16[2,16,33,256]{3,1,2,0:T(8,128)(2,1)S(1)}, u32[]{:S(2)}, u32[]{:S(2)}) collective-permute-start(bf16[2,16,33,256]{3,1,2,0:T(8,128)(2,1)S(1)} %pad_maximum_fusion.1), channel_id=1, source_target_pairs={{64,0},{72,8},{80,16},{88,24},{96,32},{104,40},{112,48},{120,56},{... | collective-permute-start | bytes 1622024 | tf_op jit(solution)/shard_map/ppermute | solution.py:16
  42.6 14.5 %collective-permute-start.4 = (bf16[2,16,33,256]{3,1,2,0:T(8,128)(2,1)S(1)}, bf16[2,16,33,256]{3,1,2,0:T(8,128)(2,1)S(1)}, u32[]{:S(2)}, u32[]{:S(2)}) collective-permute-start(bf16[2,16,33,256]{3,1,2,0:T(8,128)(2,1)S(1)} %pad_maximum_fusion.1), channel_id=1, source_target_pairs={{128,0},{136,8},{144,16},{152,24},{160,32},{168,40},{176,48},{184,... | collective-permute-start | bytes 1622024 | tf_op jit(solution)/shard_map/ppermute | solution.py:16
  43.0 26.9 %collective-permute-start.5 = (bf16[2,16,33,256]{3,1,2,0:T(8,128)(2,1)S(1)}, bf16[2,16,33,256]{3,1,2,0:T(8,128)(2,1)S(1)}, u32[]{:S(2)}, u32[]{:S(2)}) collective-permute-start(bf16[2,16,33,256]{3,1,2,0:T(8,128)(2,1)S(1)} %pad_maximum_fusion.1), channel_id=1, source_target_pairs={{192,0},{200,8},{208,16},{216,24},{224,32},{232,40},{240,48},{248,... | collective-permute-start | bytes 1622024 | tf_op jit(solution)/shard_map/ppermute | solution.py:16
  70.2 13.8 %collective-permute-start.6 = (bf16[2,16,34,256]{3,1,2,0:T(8,128)(2,1)S(1)}, bf16[2,16,34,256]{3,1,2,0:T(8,128)(2,1)S(1)}, u32[]{:S(2)}, u32[]{:S(2)}) collective-permute-start(bf16[2,16,34,256]{3,1,2,0:T(8,128)(2,1)S(1)} %pad_maximum_fusion), channel_id=1, source_target_pairs={{64,0},{72,8},{80,16},{88,24},{96,32},{104,40},{112,48},{120,56},{... | collective-permute-start | bytes 1671176 | tf_op jit(solution)/shard_map/ppermute | solution.py:16
  70.2 14.4 %collective-permute-start.7 = (bf16[2,16,34,256]{3,1,2,0:T(8,128)(2,1)S(1)}, bf16[2,16,34,256]{3,1,2,0:T(8,128)(2,1)S(1)}, u32[]{:S(2)}, u32[]{:S(2)}) collective-permute-start(bf16[2,16,34,256]{3,1,2,0:T(8,128)(2,1)S(1)} %pad_maximum_fusion), channel_id=1, source_target_pairs={{128,0},{136,8},{144,16},{152,24},{160,32},{168,40},{176,48},{184,... | collective-permute-start | bytes 1671176 | tf_op jit(solution)/shard_map/ppermute | solution.py:16
  70.7 27.6 %collective-permute-start.8 = (bf16[2,16,34,256]{3,1,2,0:T(8,128)(2,1)S(1)}, bf16[2,16,34,256]{3,1,2,0:T(8,128)(2,1)S(1)}, u32[]{:S(2)}, u32[]{:S(2)}) collective-permute-start(bf16[2,16,34,256]{3,1,2,0:T(8,128)(2,1)S(1)} %pad_maximum_fusion), channel_id=1, source_target_pairs={{192,0},{200,8},{208,16},{216,24},{224,32},{232,40},{240,48},{248,... | collective-permute-start | bytes 1671176 | tf_op jit(solution)/shard_map/ppermute | solution.py:16
  73.6 25.0 %copy-start.19 = (bf16[16,256,1]{1,0,2:T(8,128)(2,1)S(1)}, bf16[16,256,1]{1,0,2:T(8,128)(2,1)}, u32[]{:S(2)}) copy-start(bf16[16,256,1]{1,0,2:T(8,128)(2,1)} %fusion.9) | copy-start | bytes 24580
  98.5 0.7 copy-start.6
  98.6 0.9 copy-start.9
  99.5 78.1 %copy-start.10 = (f32[4096]{0:T(1024)S(1)}, f32[4096]{0:T(1024)}, u32[]{:S(2)}) copy-start(f32[4096]{0:T(1024)} %param.24) | copy-start | bytes 49156
  100.6 170.0 %all-gather.8.cloned.1.call-start = ((), (), s32[]{:S(2)}) async-start(), calls=%async_computation.1 | async-start | bytes 4325376 | tf_op jit(solution)/shard_map/all_gather | solution.py:110
  101.2 169.5 %all-gather.6.cloned.1.call-start = ((), (), s32[]{:S(2)}) async-start(), calls=%async_computation | async-start | bytes 7077888 | tf_op jit(solution)/shard_map/all_gather | solution.py:112
  175.8 43.1 %copy-start.8 = (bf16[16,4096]{1,0:T(8,128)(2,1)S(1)}, bf16[16,4096]{1,0:T(8,128)(2,1)}, u32[]{:S(2)}) copy-start(bf16[16,4096]{1,0:T(8,128)(2,1)} %get-tuple-element.11) | copy-start | bytes 393220
  179.7 66.1 %copy-start.7 = (bf16[16,4096]{1,0:T(8,128)(2,1)S(1)}, bf16[16,4096]{1,0:T(8,128)(2,1)}, u32[]{:S(2)}) copy-start(bf16[16,4096]{1,0:T(8,128)(2,1)} %get-tuple-element.10) | copy-start | bytes 393220
  217.7 28.1 %copy-start.23 = (f32[16]{0:T(128)S(1)}, f32[16]{0:T(128)}, u32[]{:S(2)}) copy-start(f32[16]{0:T(128)} %get-tuple-element.3) | copy-start | bytes 196
  270.6 7.6 %copy-start.12 = (bf16[16,256]{1,0:T(8,128)(2,1)S(1)}, bf16[16,256]{1,0:T(8,128)(2,1)}, u32[]{:S(2)}) copy-start(bf16[16,256]{1,0:T(8,128)(2,1)} %reshape.403) | copy-start | bytes 24580
  270.6 7.6 %copy-start.18 = (pred[768]{0:T(1024)(128)(4,1)S(1)}, pred[768]{0:T(1024)(128)(4,1)}, u32[]{:S(2)}) copy-start(pred[768]{0:T(1024)(128)(4,1)} %iota_compare_fusion.2) | copy-start | bytes 2308
  270.6 32.9 %copy-start.11 = (bf16[16,256]{1,0:T(8,128)(2,1)S(1)}, bf16[16,256]{1,0:T(8,128)(2,1)}, u32[]{:S(2)}) copy-start(bf16[16,256]{1,0:T(8,128)(2,1)} %reshape.398) | copy-start | bytes 24580
Sparse Core Ops, SparseCore 0:
  100.7 74.9 all-reduce.2
Sparse Core Ops, SparseCore 1:
  103.7 52.1 all-gather.7
  157.5 73.3 all-gather.5
where the time goes:
time: 360 us
  blocking collectives  156 us (43%)
  waiting for transfers between devices  136 us (38%)
  matrix products  30.7 us (9%)
  between operations  16.7 us (5%)
  other arithmetic  8.37 us (2%)
  starting transfers between devices  7.79 us (2%)
  local copies, waits for them, and re-layouts  4.05 us (1%)
    all_gather x3, blocking collectives, shards(): every_query = lax.all_gather(cross_query, 'hyp', axis=0, tiled=True)  84.7 us
    psum x1, waiting for transfers between devices, shards(): lax.psum(partial_out.astype(jnp.bfloat16), 'head').astype(jnp.float32)  72.8 us
    all_gather x3, blocking collectives, shards(): every_answer = lax.all_gather(answer, 'hyp', axis=0, tiled=True)  71.4 us
    ppermute x9, waiting for transfers between devices, shifted(): return lax.ppermute(block, axis, route)  62.5 us
    ppermute x9, starting transfers between devices, shifted(): return lax.ppermute(block, axis, route)  7.67 us
    dot_general x1, matrix products, shards(): jnp.dot(lax.all_gather(encoder_rows, 'head', axis=1, tiled=True), full_we...  7.47 us
  transfers between devices with their start and end apart: 12, of which 9 were waited for; matrix products, arithmetic and copies ran while one was open for 7% of the time, Pallas kernels for 0%

commit v1 on v0

--- a/solution.py
+++ b/solution.py
@@ -148,9 +148,9 @@
             .astype(jnp.bfloat16)
         )
         partial_out = jnp.dot(self_context, self_wo, preferred_element_type=jnp.float32)
-        residual = hidden_in + lax.psum(partial_out.astype(jnp.bfloat16), "head").astype(
-            jnp.float32
-        )
+        residual = hidden_in + jnp.sum(
+            lax.all_gather(partial_out.astype(jnp.bfloat16), "head"), axis=0
+        ).astype(jnp.float32)
         normed_cross = rms_scaled(residual, cross_gain).astype(jnp.bfloat16)
         cross_query = jnp.dot(normed_cross, cross_wq, preferred_element_type=jnp.float32).astype(
             jnp.bfloat16

time: 360 us -> 385 us (1.069)
  waiting for transfers between devices: 136 us -> 159 us
  other arithmetic: 8.37 us -> 17.5 us
  blocking collectives: 156 us -> 150 us
    psum x1 -> x0, waiting for transfers between devices: 72.8 us -> none  [shards(): lax.psum(partial_out.astype(jnp.bfloat16), 'head').astype(jnp.float32)]
    all_gather x0 -> x3, waiting for transfers between devices: none -> 51.3 us  [shards(): lax.all_gather(partial_out.astype(jnp.bfloat16), 'head')]
    all_gather x1, waiting for transfers between devices: 0.02 us -> 46.2 us  [shards(): lax.all_gather(encoder_rows, 'head', axis=1, tiled=True)]
    all_gather x3, blocking collectives: 84.7 us -> 77.2 us  [shards(): every_query = lax.all_gather(cross_query, 'hyp', axis=0, tiled=True)]
    reduce_sum x0 -> x3, other arithmetic: none -> 4.15 us  [shards(): jnp.sum(lax.all_gather(partial_out.astype(jnp.bfloat16), 'head'), axis=0)]
  transfers between devices with their start and end apart: 12 -> 14, of which waited for: 9 -> 11; matrix products, arithmetic and copies ran while one was open for 7% -> 9% of each run, Pallas kernels for 0% -> 0%
where the time goes in v1:
time: 385 us; the launch traced here: 384 us
  waiting for transfers between devices  159 us (41%)
  blocking collectives  150 us (39%)
  matrix products  31.8 us (8%)
  other arithmetic  17.5 us (5%)
  between operations  14.9 us (4%)
  starting transfers between devices  7.91 us (2%)
    all_gather x3, blocking collectives, shards(): every_query = lax.all_gather(cross_query, 'hyp', axis=0, tiled=True)  77.2 us
    all_gather x3, blocking collectives, shards(): every_answer = lax.all_gather(answer, 'hyp', axis=0, tiled=True)  72.8 us
    ppermute x9, waiting for transfers between devices, shifted(): return lax.ppermute(block, axis, route)  60.1 us
    all_gather x3, waiting for transfers between devices, shards(): lax.all_gather(partial_out.astype(jnp.bfloat16), 'head')  51.3 us
    all_gather x1, waiting for transfers between devices, shards(): lax.all_gather(encoder_rows, 'head', axis=1, tiled=True)  46.2 us
  transfers between devices with their start and end apart: 14, of which 11 were waited for; matrix products, arithmetic and copies ran while one was open for 9% of the time, Pallas kernels for 0%

profile of v1, /device:TPU:1, one launch (start us, length us, event | category | flops | bytes accessed | tf_op | source)
XLA Modules:
  0.0 384.1 jit_solution(11741894073573335906)
XLA Ops:
  7.3 1.5 copy_bitcast_fusion
  8.8 0.7 copy-done.5
  9.4 0.8 pad_maximum_fusion.2
  10.3 3.6 collective-permute-start
  13.8 0.3 collective-permute-start.1
  14.2 0.7 collective-permute-start.2
  15.1 0.4 multiply_reduce_fusion.1
  15.8 2.7 fusion.11
  18.5 1.0 fusion.10
  19.5 0.4 fusion.8
  19.9 0.4 fusion.7
  20.3 0.4 fusion.5
  20.7 0.4 fusion.4
  21.1 2.6 fusion.3
  23.7 0.6 maximum_bitcast_fusion.1
  24.3 0.6 broadcast_compare_fusion.6
  24.9 0.5 broadcast_compare_fusion.4
  25.5 10.4 %collective-permute-done = bf16[2,16,32,256]{3,1,2,0:T(8,128)(2,1)} collective-permute-done((bf16[2,16,32,256]{3,1,2,0:T(8,128)(2,1)}, bf16[2,16,32,256]{3,1,2,0:T(8,128)(2,1)}, u32[]{:S(2)}, u32[]{:S(2)}) %collective-permute-start) | collective-permute-done | bytes 524320 | tf_op jit(solution)/shard_map/ppermute | solution.py:16
  35.9 4.9 %collective-permute-done.2 = bf16[2,16,32,256]{3,1,2,0:T(8,128)(2,1)} collective-permute-done((bf16[2,16,32,256]{3,1,2,0:T(8,128)(2,1)}, bf16[2,16,32,256]{3,1,2,0:T(8,128)(2,1)}, u32[]{:S(2)}, u32[]{:S(2)}) %collective-permute-start.2) | collective-permute-done | bytes 524320 | tf_op jit(solution)/shard_map/ppermute | solution.py:16
  40.7 1.5 select_select_fusion.2
  42.3 0.8 pad_maximum_fusion.1
  43.1 0.3 collective-permute-start.4
  43.5 1.1 collective-permute-start.5
  45.4 1.1 convolution_convert_fusion.2
  46.6 2.0 fusion.6
  48.6 8.2 %collective-permute-done.3 = bf16[2,16,33,256]{3,1,2,0:T(8,128)(2,1)} collective-permute-done((bf16[2,16,33,256]{3,1,2,0:T(8,128)(2,1)}, bf16[2,16,33,256]{3,1,2,0:T(8,128)(2,1)}, u32[]{:S(2)}, u32[]{:S(2)}) %collective-permute-start.3) | collective-permute-done | bytes 540704 | tf_op jit(solution)/shard_map/ppermute | solution.py:16
  56.8 0.9 collective-permute-done.4
  57.7 13.0 %collective-permute-done.5 = bf16[2,16,33,256]{3,1,2,0:T(8,128)(2,1)} collective-permute-done((bf16[2,16,33,256]{3,1,2,0:T(8,128)(2,1)}, bf16[2,16,33,256]{3,1,2,0:T(8,128)(2,1)}, u32[]{:S(2)}, u32[]{:S(2)}) %collective-permute-start.5) | collective-permute-done | bytes 540704 | tf_op jit(solution)/shard_map/ppermute | solution.py:16
  70.7 1.5 select_select_fusion.1
  72.3 0.9 pad_maximum_fusion
  73.2 0.3 collective-permute-start.7
  73.5 1.1 collective-permute-start.8
  75.5 1.1 convolution_convert_fusion.1
  76.8 2.0 fusion.9
  78.8 8.3 %collective-permute-done.6 = bf16[2,16,34,256]{3,1,2,0:T(8,128)(2,1)} collective-permute-done((bf16[2,16,34,256]{3,1,2,0:T(8,128)(2,1)}, bf16[2,16,34,256]{3,1,2,0:T(8,128)(2,1)}, u32[]{:S(2)}, u32[]{:S(2)}) %collective-permute-start.6) | collective-permute-done | bytes 557088 | tf_op jit(solution)/shard_map/ppermute | solution.py:16
  87.1 0.5 collective-permute-done.7
  87.6 13.9 %collective-permute-done.8 = bf16[2,16,34,256]{3,1,2,0:T(8,128)(2,1)} collective-permute-done((bf16[2,16,34,256]{3,1,2,0:T(8,128)(2,1)}, bf16[2,16,34,256]{3,1,2,0:T(8,128)(2,1)}, u32[]{:S(2)}, u32[]{:S(2)}) %collective-permute-start.8) | collective-permute-done | bytes 557088 | tf_op jit(solution)/shard_map/ppermute | solution.py:16
  101.5 1.6 select_select_fusion
  104.1 1.1 convolution_convert_fusion
  105.2 0.5 all-gather.14.cloned.1.call-update
  105.8 0.5 all-gather.12.cloned.1.call-update
  107.0 0.6 iota_compare_fusion.2
  107.6 1.4 reduce_sum.146
  109.0 14.0 %all-gather.18.cloned.1.call-done = bf16[128,4096]{1,0:T(8,128)(2,1)} async-done(((bf16[16,4096]{1,0:T(8,128)(2,1)}), bf16[128,4096]{1,0:T(8,128)(2,1)}) %all-gather.18.cloned.1.call-update) | async-done | bytes 1048592 | tf_op jit(solution)/shard_map/all_gather | solution.py:152
  123.0 1.4 reduce_sum.151
  124.4 37.3 %all-gather.20.cloned.1.call-done = bf16[128,4096]{1,0:T(8,128)(2,1)} async-done(((bf16[16,4096]{1,0:T(8,128)(2,1)}), bf16[128,4096]{1,0:T(8,128)(2,1)}) %all-gather.20.cloned.1.call-update) | async-done | bytes 1048592 | tf_op jit(solution)/shard_map/all_gather | solution.py:152
  161.7 1.4 reduce_sum.156
  163.1 0.8 multiply_reduce_fusion.4
  163.9 2.0 convolution_convert_fusion.4
  165.9 30.4 %all_gather.54 = bf16[512,256]{1,0:T(8,128)(2,1)S(1)} all-gather(bf16[16,256]{1,0:T(8,128)(2,1)S(1)} %convolution_convert_fusion.4), channel_id=1, replica_groups=mesh['hyp'=32,'head'=8] {'hyp'}, dimensions={0}, use_global_device_ids=true | all-gather | bytes 270336 | tf_op jit(solution)/shard_map/all_gather | solution.py:158
  196.4 0.6 add_rsqrt_fusion.2
  197.0 2.0 convolution_convert_fusion.8
  199.0 24.2 %all_gather.50 = bf16[512,256]{1,0:T(8,128)(2,1)S(1)} all-gather(bf16[16,256]{1,0:T(8,128)(2,1)S(1)} %convolution_convert_fusion.8), channel_id=1, replica_groups=mesh['hyp'=32,'head'=8] {'hyp'}, dimensions={0}, use_global_device_ids=true | all-gather | bytes 270336 | tf_op jit(solution)/shard_map/all_gather | solution.py:158
  223.4 2.0 convolution_convert_fusion.12
  225.4 22.6 %all_gather.46 = bf16[512,256]{1,0:T(8,128)(2,1)S(1)} all-gather(bf16[16,256]{1,0:T(8,128)(2,1)S(1)} %convolution_convert_fusion.12), channel_id=1, replica_groups=mesh['hyp'=32,'head'=8] {'hyp'}, dimensions={0}, use_global_device_ids=true | all-gather | bytes 270336 | tf_op jit(solution)/shard_map/all_gather | solution.py:158
  248.1 46.2 %all-gather.12.cloned.1.call-done = bf16[768,4096]{1,0:T(8,128)(2,1)} async-done(((bf16[768,512]{1,0:T(8,128)(2,1)}), bf16[768,4096]{1,0:T(8,128)(2,1)}) %all-gather.12.cloned.1.call-update) | async-done | bytes 6291472 | tf_op jit(solution)/shard_map/all_gather | solution.py:112
  294.3 7.5 %convolution_convert_fusion.3 = bf16[768,512]{0,1:T(8,128)(2,1)S(1)} fusion(bf16[768,4096]{1,0:T(8,128)(2,1)} %all-gather.12.cloned.1.call-done, bf16[4096,512]{1,0:T(8,128)(2,1)} %all-gather.14.cloned.1.call-done), kind=kOutput, calls=%fused_computation.3 | convolution fusion | flops 3221618688 | bytes 11272192 | tf_op jit(solution)/shard_map/dot_general | solution.py:111
  301.8 0.3 fusion.77
  302.5 25.8 %all-gather.5 = bf16[512,1,256]{2,0,1:T(8,128)(2,1)S(1)} all-gather(bf16[16,1,256]{2,0,1:T(8,128)(2,1)S(1)} %fusion.14), channel_id=7, replica_groups=mesh['hyp'=32,'head'=8] {'hyp'}, dimensions={0}, use_global_device_ids=true | all-gather | bytes 270336 | tf_op jit(solution)/shard_map/all_gather | solution.py:168
  328.4 0.3 fusion.78
  329.1 24.2 %all-gather.3 = bf16[512,1,256]{2,0,1:T(8,128)(2,1)S(1)} all-gather(bf16[16,1,256]{2,0,1:T(8,128)(2,1)S(1)} %fusion.13), channel_id=5, replica_groups=mesh['hyp'=32,'head'=8] {'hyp'}, dimensions={0}, use_global_device_ids=true | all-gather | bytes 270336 | tf_op jit(solution)/shard_map/all_gather | solution.py:168
  353.4 0.3 fusion.79
  354.1 22.7 %all-gather.1 = bf16[512,1,256]{2,0,1:T(8,128)(2,1)S(1)} all-gather(bf16[16,1,256]{2,0,1:T(8,128)(2,1)S(1)} %fusion.12), channel_id=3, replica_groups=mesh['hyp'=32,'head'=8] {'hyp'}, dimensions={0}, use_global_device_ids=true | all-gather | bytes 270336 | tf_op jit(solution)/shard_map/all_gather | solution.py:168
  377.0 0.6 pad_maximum_fusion.4
  (120 shorter events, 5.4 us)
Async XLA Ops:
  7.2 38.3 %copy-start = (bf16[256,4096]{1,0:T(8,128)(2,1)S(1)}, bf16[256,4096]{1,0:T(8,128)(2,1)}, u32[]{:S(2)}) copy-start(bf16[256,4096]{1,0:T(8,128)(2,1)} %param.23) | copy-start | bytes 6291460
  7.2 7.7 %copy-start.23 = (s32[32,4]{0,1:T(4,128)S(1)}, s32[32,4]{0,1:T(4,128)}, u32[]{:S(2)}) copy-start(s32[32,4]{0,1:T(4,128)} %param.18) | copy-start | bytes 1540
  7.2 7.9 %copy-start.3 = (bf16[3,16,4096]{2,1,0:T(8,128)(2,1)S(1)}, bf16[3,16,4096]{2,1,0:T(8,128)(2,1)}, u32[]{:S(2)}) copy-start(bf16[3,16,4096]{2,1,0:T(8,128)(2,1)} %param.16) | copy-start | bytes 1179652
  7.2 7.9 %copy-start.27 = (bf16[8,4096]{1,0:T(8,128)(2,1)S(1)}, bf16[8,4096]{1,0:T(8,128)(2,1)}, u32[]{:S(2)}) copy-start(bf16[8,4096]{1,0:T(8,128)(2,1)} %param.17) | copy-start | bytes 196612
  7.2 8.4 %copy-start.19 = (f32[4096]{0:T(1024)S(1)}, f32[4096]{0:T(1024)}, u32[]{:S(2)}) copy-start(f32[4096]{0:T(1024)} %param.19) | copy-start | bytes 49156
  7.2 100.4 %all-gather.16.cloned.1.call-start = ((), (), s32[]{:S(2)}) async-start(), calls=%async_computation.2 | async-start | bytes 1179648 | tf_op jit(solution)/shard_map/all_gather | solution.py:152
  8.7 0.7 copy-start.5
  8.8 1.5 copy-start.7
  10.3 25.6 %collective-permute-start = (bf16[2,16,32,256]{3,1,2,0:T(8,128)(2,1)}, bf16[2,16,32,256]{3,1,2,0:T(8,128)(2,1)}, u32[]{:S(2)}, u32[]{:S(2)}) collective-permute-start(bf16[2,16,32,256]{3,1,2,0:T(8,128)(2,1)} %pad_maximum_fusion.2), channel_id=1, source_target_pairs={{64,0},{72,8},{80,16},{88,24},{96,32},{104,40},{112,48},{120,56},{... | collective-permute-start | bytes 1572872 | tf_op jit(solution)/shard_map/ppermute | solution.py:16
  13.8 22.0 %collective-permute-start.1 = (bf16[2,16,32,256]{3,1,2,0:T(8,128)(2,1)}, bf16[2,16,32,256]{3,1,2,0:T(8,128)(2,1)}, u32[]{:S(2)}, u32[]{:S(2)}) collective-permute-start(bf16[2,16,32,256]{3,1,2,0:T(8,128)(2,1)} %pad_maximum_fusion.2), channel_id=1, source_target_pairs={{128,0},{136,8},{144,16},{152,24},{160,32},{168,40},{176,48},{184,... | collective-permute-start | bytes 1572872 | tf_op jit(solution)/shard_map/ppermute | solution.py:16
  14.2 26.6 %collective-permute-start.2 = (bf16[2,16,32,256]{3,1,2,0:T(8,128)(2,1)}, bf16[2,16,32,256]{3,1,2,0:T(8,128)(2,1)}, u32[]{:S(2)}, u32[]{:S(2)}) collective-permute-start(bf16[2,16,32,256]{3,1,2,0:T(8,128)(2,1)} %pad_maximum_fusion.2), channel_id=1, source_target_pairs={{192,0},{200,8},{208,16},{216,24},{224,32},{232,40},{240,48},{248,... | collective-permute-start | bytes 1572872 | tf_op jit(solution)/shard_map/ppermute | solution.py:16
  15.1 3.4 copy-start.2
  15.8 4.1 %copy-start.9 = (bf16[16,4096]{1,0:T(8,128)(2,1)}, bf16[16,4096]{1,0:T(8,128)(2,1)S(1)}, u32[]{:S(2)}) copy-start(bf16[16,4096]{1,0:T(8,128)(2,1)S(1)} %get-tuple-element.22) | copy-start | bytes 393220
  15.8 3.7 copy-start.1
  20.3 0.8 copy-start.22
  20.7 20.1 %copy-start.6 = (bf16[1,16,32,256]{3,1,2,0:T(8,128)(2,1)S(1)}, bf16[1,16,32,256]{3,1,2,0:T(8,128)(2,1)}, u32[]{:S(2)}) copy-start(bf16[1,16,32,256]{3,1,2,0:T(8,128)(2,1)} %copy-done.5) | copy-start | bytes 786436
  20.7 20.1 %copy-start.8 = (bf16[1,16,32,256]{3,1,2,0:T(8,128)(2,1)S(1)}, bf16[1,16,32,256]{3,1,2,0:T(8,128)(2,1)}, u32[]{:S(2)}) copy-start(bf16[1,16,32,256]{3,1,2,0:T(8,128)(2,1)} %copy-done.7) | copy-start | bytes 786436
  24.3 20.4 %copy-start.15 = (bf16[2,16,1,256]{3,1,2,0:T(8,128)(2,1)}, bf16[2,16,1,256]{3,1,2,0:T(8,128)(2,1)S(1)}, u32[]{:S(2)}) copy-start(bf16[2,16,1,256]{3,1,2,0:T(8,128)(2,1)S(1)} %maximum_bitcast_fusion) | copy-start | bytes 49156
  40.7 3.9 %copy-start.21 = (bf16[16,256,1]{1,0,2:T(8,128)(2,1)S(1)}, bf16[16,256,1]{1,0,2:T(8,128)(2,1)}, u32[]{:S(2)}) copy-start(bf16[16,256,1]{1,0,2:T(8,128)(2,1)} %fusion.3) | copy-start | bytes 24580
  43.1 3.5 copy-start.10
  43.1 13.7 %collective-permute-start.3 = (bf16[2,16,33,256]{3,1,2,0:T(8,128)(2,1)}, bf16[2,16,33,256]{3,1,2,0:T(8,128)(2,1)}, u32[]{:S(2)}, u32[]{:S(2)}) collective-permute-start(bf16[2,16,33,256]{3,1,2,0:T(8,128)(2,1)} %pad_maximum_fusion.1), channel_id=1, source_target_pairs={{64,0},{72,8},{80,16},{88,24},{96,32},{104,40},{112,48},{120,56},{... | collective-permute-start | bytes 1622024 | tf_op jit(solution)/shard_map/ppermute | solution.py:16
  43.1 14.6 %collective-permute-start.4 = (bf16[2,16,33,256]{3,1,2,0:T(8,128)(2,1)}, bf16[2,16,33,256]{3,1,2,0:T(8,128)(2,1)}, u32[]{:S(2)}, u32[]{:S(2)}) collective-permute-start(bf16[2,16,33,256]{3,1,2,0:T(8,128)(2,1)} %pad_maximum_fusion.1), channel_id=1, source_target_pairs={{128,0},{136,8},{144,16},{152,24},{160,32},{168,40},{176,48},{184,... | collective-permute-start | bytes 1622024 | tf_op jit(solution)/shard_map/ppermute | solution.py:16
  43.5 27.3 %collective-permute-start.5 = (bf16[2,16,33,256]{3,1,2,0:T(8,128)(2,1)}, bf16[2,16,33,256]{3,1,2,0:T(8,128)(2,1)}, u32[]{:S(2)}, u32[]{:S(2)}) collective-permute-start(bf16[2,16,33,256]{3,1,2,0:T(8,128)(2,1)} %pad_maximum_fusion.1), channel_id=1, source_target_pairs={{192,0},{200,8},{208,16},{216,24},{224,32},{232,40},{240,48},{248,... | collective-permute-start | bytes 1622024 | tf_op jit(solution)/shard_map/ppermute | solution.py:16
  46.5 76.5 %all-gather.18.cloned.1.call-start = ((), (), s32[]{:S(2)}) async-start(), calls=%async_computation.3 | async-start | bytes 1179648 | tf_op jit(solution)/shard_map/all_gather | solution.py:152
  46.6 25.7 %copy-start.13 = (bf16[2,16,1,256]{3,1,2,0:T(8,128)(2,1)S(1)}, bf16[2,16,1,256]{3,1,2,0:T(8,128)(2,1)}, u32[]{:S(2)}) copy-start(bf16[2,16,1,256]{3,1,2,0:T(8,128)(2,1)} %maximum_bitcast_fusion.1) | copy-start | bytes 49156
  73.2 14.0 %collective-permute-start.6 = (bf16[2,16,34,256]{3,1,2,0:T(8,128)(2,1)}, bf16[2,16,34,256]{3,1,2,0:T(8,128)(2,1)}, u32[]{:S(2)}, u32[]{:S(2)}) collective-permute-start(bf16[2,16,34,256]{3,1,2,0:T(8,128)(2,1)} %pad_maximum_fusion), channel_id=1, source_target_pairs={{64,0},{72,8},{80,16},{88,24},{96,32},{104,40},{112,48},{120,56},{... | collective-permute-start | bytes 1671176 | tf_op jit(solution)/shard_map/ppermute | solution.py:16
  73.2 14.4 %collective-permute-start.7 = (bf16[2,16,34,256]{3,1,2,0:T(8,128)(2,1)}, bf16[2,16,34,256]{3,1,2,0:T(8,128)(2,1)}, u32[]{:S(2)}, u32[]{:S(2)}) collective-permute-start(bf16[2,16,34,256]{3,1,2,0:T(8,128)(2,1)} %pad_maximum_fusion), channel_id=1, source_target_pairs={{128,0},{136,8},{144,16},{152,24},{160,32},{168,40},{176,48},{184,... | collective-permute-start | bytes 1671176 | tf_op jit(solution)/shard_map/ppermute | solution.py:16
  73.5 28.0 %collective-permute-start.8 = (bf16[2,16,34,256]{3,1,2,0:T(8,128)(2,1)}, bf16[2,16,34,256]{3,1,2,0:T(8,128)(2,1)}, u32[]{:S(2)}, u32[]{:S(2)}) collective-permute-start(bf16[2,16,34,256]{3,1,2,0:T(8,128)(2,1)} %pad_maximum_fusion), channel_id=1, source_target_pairs={{192,0},{200,8},{208,16},{216,24},{224,32},{232,40},{240,48},{248,... | collective-permute-start | bytes 1671176 | tf_op jit(solution)/shard_map/ppermute | solution.py:16
  75.4 3.3 copy-start.17
  75.4 3.3 copy-start.18
  75.4 3.4 copy-start.26
  75.4 26.1 %copy-start.14 = (bf16[2,16,1,256]{3,1,2,0:T(8,128)(2,1)S(1)}, bf16[2,16,1,256]{3,1,2,0:T(8,128)(2,1)}, u32[]{:S(2)}) copy-start(bf16[2,16,1,256]{3,1,2,0:T(8,128)(2,1)} %maximum_bitcast_fusion.1) | copy-start | bytes 49156
  75.5 26.1 %copy-start.24 = (pred[16]{0:T(512)(128)(4,1)S(1)}, pred[16]{0:T(512)(128)(4,1)}, u32[]{:S(2)}) copy-start(pred[16]{0:T(512)(128)(4,1)} %get-tuple-element.15) | copy-start | bytes 52
  76.6 85.1 %all-gather.20.cloned.1.call-start = ((), (), s32[]{:S(2)}) async-start(), calls=%async_computation.4 | async-start | bytes 1179648 | tf_op jit(solution)/shard_map/all_gather | solution.py:152
  103.1 0.7 copy-start.11
  103.1 0.9 copy-start.12
  105.2 143.0 %all-gather.14.cloned.1.call-start = ((), (), s32[]{:S(2)}) async-start(), calls=%async_computation.1 | async-start | bytes 4325376 | tf_op jit(solution)/shard_map/all_gather | solution.py:110
  105.8 57.3 %copy-start.4 = (bf16[3,16,4096]{2,1,0:T(8,128)(2,1)S(1)}, bf16[3,16,4096]{2,1,0:T(8,128)(2,1)}, u32[]{:S(2)}) copy-start(bf16[3,16,4096]{2,1,0:T(8,128)(2,1)} %param.16) | copy-start | bytes 1179652
  105.8 188.5 %all-gather.12.cloned.1.call-start = ((), (), s32[]{:S(2)}) async-start(), calls=%async_computation | async-start | bytes 7077888 | tf_op jit(solution)/shard_map/all_gather | solution.py:112
  107.6 56.3 %copy-start.16 = (f32[4096]{0:T(1024)S(1)}, f32[4096]{0:T(1024)}, u32[]{:S(2)}) copy-start(f32[4096]{0:T(1024)} %param.24) | copy-start | bytes 49156
  196.4 27.0 %copy-start.25 = (f32[16]{0:T(128)S(1)}, f32[16]{0:T(128)}, u32[]{:S(2)}) copy-start(f32[16]{0:T(128)} %get-tuple-element.3) | copy-start | bytes 196
  248.1 53.7 %copy-start.20 = (pred[768]{0:T(1024)(128)(4,1)S(1)}, pred[768]{0:T(1024)(128)(4,1)}, u32[]{:S(2)}) copy-start(pred[768]{0:T(1024)(128)(4,1)} %iota_compare_fusion.2) | copy-start | bytes 2308
Sparse Core Ops, SparseCore 0:
  46.7 38.6 all-gather.15
  87.2 35.8 all-gather.17
  124.8 36.8 all-gather.19
  164.1 55.0 all-gather.13
  220.8 73.4 all-gather.11
